TPU v7x, 32 devices: a whole 2x2x4 slice. The times are simulated.
32 devices in a mesh: dp: 4 (over y, core), mp: 8 (over z, x).
Axes of the slice: x: 2, y: 2, z: 4, core: 2. Of those that a mesh axis runs over, the one named last changes fastest.
Arguments:
- tokens: bfloat16 [512, 6144], P('dp', 'mp'), may hold values from -6 to 6
- norm_gain: bfloat16 [6144], P('mp'), may hold values from 0.5 to 1.5
- qkv_weight: bfloat16 [3, 128, 24, 6144], P(None, 'mp', None, 'dp'), may hold values from -0.078125 to 0.078125
- head_weight: bfloat16 [128, 24, 6144], P('mp', None, 'dp'), may hold values from -0.109375 to 0.109375
- up_weight: bfloat16 [12288, 6144], P('mp', 'dp'), may hold values from -0.078125 to 0.078125
- down_weight: bfloat16 [12288, 6144], P('mp', 'dp'), may hold values from -0.0546875 to 0.0546875
- cotangent: bfloat16 [512, 6144], P('dp', 'mp'), may hold values from -6 to 6
Outputs:
- mixed: bfloat16 [512, 6144], P('dp', 'mp')
- tokens_grad: float32 [512, 6144], P('dp', 'mp')
- qkv_grad: bfloat16 [3, 128, 24, 6144], P(None, 'mp', None, 'dp')
- head_grad: bfloat16 [128, 24, 6144], P('mp', None, 'dp')
- up_grad: bfloat16 [12288, 6144], P('mp', 'dp')
- down_grad: bfloat16 [12288, 6144], P('mp', 'dp')
- gain_grad: float32 [6144], P('mp')
All inputs are finite; a program needn't handle non-finite values.
Results may differ from a plain program's by a relative error of at most 0.013.
Values may be sent and summed in bfloat16 or wider, within the bound.
No kernel may reach another device: no remote copies, remote signals or barrier semaphores. Data moves between devices by JAX's collectives and lax.ppermute only.
A program may use at most 256 MiB of HBM per device.

v0:
```python
import math
import jax
import jax.numpy as jnp
from jax import lax
from jax.sharding import PartitionSpec as P

D = 6144
HEADS = 24
HS = 128
PATCHES = 128
QB = 8
IMG_DP = 1
ROWS = 128
TQ = 16
ITEMS = 192
epsilon = 1e-06
contract_rows = (((0,), (0,)), ((), ()))
contract_cols = (((1,), (1,)), ((), ()))


def gelu_pair(inputs):
    normal_cdf = 0.5 * (1.0 + jax.scipy.special.erf(inputs * 0.7071067811865476))
    density = jnp.exp(-0.5 * inputs * inputs) * 0.3989422804014327
    return (inputs * normal_cdf, normal_cdf + inputs * density)


def head_norm(values):
    center = values - jnp.mean(values, axis=0, keepdims=True)
    inverse = lax.rsqrt(jnp.mean(center * center, axis=0, keepdims=True) + epsilon)
    return (center * inverse, inverse)


def norm_back(upstream, normed, inverse):
    return inverse * (
        upstream
        - jnp.mean(upstream, axis=0, keepdims=True)
        - normed * jnp.mean(upstream * normed, axis=0, keepdims=True)
    )


def to_items(pair_rows):
    depth = pair_rows.shape[1]
    shaped = pair_rows.reshape(2, depth, HEADS, IMG_DP, 1, PATCHES)
    spread = jnp.broadcast_to(shaped, (2, depth, HEADS, IMG_DP, QB, PATCHES))
    return jnp.transpose(spread, (1, 2, 3, 4, 0, 5)).reshape(depth, HEADS * IMG_DP * QB, 2, PATCHES)


def from_items(pair_items):
    depth = pair_items.shape[0]
    shaped = pair_items.reshape(depth, HEADS, IMG_DP, QB, 2, PATCHES)
    summed = jnp.sum(shaped.astype(jnp.float32), axis=3).astype(jnp.bfloat16)
    return jnp.transpose(summed, (3, 0, 1, 2, 4)).reshape(2, depth, HEADS, IMG_DP * PATCHES)


def attend(queries, keyvals):
    query_hat, query_scale = head_norm(queries.astype(jnp.float32))
    key_hat, key_scale = head_norm(keyvals[:, :, 0].astype(jnp.float32))
    query_norm = query_hat.astype(jnp.bfloat16)
    key_norm = key_hat.astype(jnp.bfloat16)
    factor = 1.0 / math.sqrt(queries.shape[0])
    scores = (
        jnp.einsum("cia,cib->iab", query_norm, key_norm, preferred_element_type=jnp.float32)
        * factor
    )
    raised = jnp.exp(scores)
    shares = raised / jnp.sum(raised, axis=2, keepdims=True)
    rounded = shares.astype(jnp.bfloat16)
    values = keyvals[:, :, 1]
    attended = jnp.einsum(
        "iab,cib->cia", rounded, values, preferred_element_type=jnp.float32
    ).astype(jnp.bfloat16)
    stored = (
        query_hat,
        query_scale,
        key_hat,
        key_scale,
        query_norm,
        key_norm,
        shares,
        rounded,
        values,
    )
    return (attended, stored)


def attend_back(upstream, stored):
    query_hat, query_scale, key_hat, key_scale, query_norm, key_norm, shares, rounded, values = (
        stored
    )
    factor = 1.0 / math.sqrt(upstream.shape[0])
    share_grad = jnp.einsum("cia,cib->iab", upstream, values, preferred_element_type=jnp.float32)
    value_grad = jnp.einsum("iab,cia->cib", rounded, upstream, preferred_element_type=jnp.float32)
    score_grad = (
        shares * (share_grad - jnp.sum(shares * share_grad, axis=2, keepdims=True)) * factor
    ).astype(jnp.bfloat16)
    query_back = jnp.einsum(
        "iab,cib->cia", score_grad, key_norm, preferred_element_type=jnp.float32
    )
    key_back = jnp.einsum(
        "iab,cia->cib", score_grad, query_norm, preferred_element_type=jnp.float32
    )
    query_grad = norm_back(query_back, query_hat, query_scale).astype(jnp.bfloat16)
    key_grad = norm_back(key_back, key_hat, key_scale).astype(jnp.bfloat16)
    pair_grad = jnp.stack([key_grad, value_grad.astype(jnp.bfloat16)], axis=2)
    return (query_grad, pair_grad)


def swap_pairs(n_dp, n_mp):
    ratio = n_mp // n_dp
    pairs = []
    for row in range(n_dp):
        for col in range(n_mp):
            owner, part = divmod(col, ratio)
            pairs.append((row * n_mp + col, owner * n_mp + row * ratio + part))
    return pairs


def swap(block):
    n_dp, n_mp = (lax.axis_size("dp"), lax.axis_size("mp"))
    return lax.ppermute(block, ("dp", "mp"), swap_pairs(n_dp, n_mp))


def spread_quarter(block):
    n_dp, n_mp = (lax.axis_size("dp"), lax.axis_size("mp"))
    ratio = n_mp // n_dp
    rows, width = block.shape
    pieces = lax.all_gather(swap(block), "mp", axis=0, tiled=False)
    pieces = pieces.reshape(n_dp, ratio, rows, width)
    return jnp.transpose(pieces, (0, 2, 1, 3)).reshape(n_dp * rows, ratio * width)


def gather_quarter(partial, rows):
    n_dp, n_mp = (lax.axis_size("dp"), lax.axis_size("mp"))
    ratio = n_mp // n_dp
    width = partial.shape[1] // ratio
    pieces = partial.reshape(n_dp, rows, ratio, width)
    pieces = jnp.transpose(pieces, (0, 2, 1, 3)).reshape(n_mp, rows, width)
    summed = lax.psum_scatter(pieces, "mp", scatter_dimension=0, tiled=True)
    return swap(summed.reshape(rows, width))


def blockwise_grad(left, right, n_blocks):
    rows = left.shape[1] // n_blocks
    total = None
    for block in range(n_blocks):
        piece = (
            jnp.dot(
                left[:, block * rows : (block + 1) * rows],
                right[block * rows : (block + 1) * rows],
                preferred_element_type=jnp.float32,
            )
            .astype(jnp.bfloat16)
            .astype(jnp.float32)
        )
        total = piece if total is None else total + piece
    return total.astype(jnp.bfloat16)


def shards(tokens, norm_gain, qkv_weight, head_weight, up_weight, down_weight, cotangent):
    n_dp, n_mp = (lax.axis_size("dp"), lax.axis_size("mp"))
    head_slice = HS // n_mp
    quarter = qkv_weight.shape[-1]
    rows, width = tokens.shape
    qkv_flat = qkv_weight.reshape(-1, quarter)
    head_flat = head_weight.reshape(-1, quarter)
    widened = tokens.astype(jnp.float32)
    block_mean = jnp.mean(widened, axis=1)
    block_center = widened - block_mean[:, None]
    block_m2 = jnp.sum(block_center * block_center, axis=1)
    stats = lax.all_gather(jnp.stack([block_mean, block_m2]), "mp", axis=0, tiled=False)
    row_mean = jnp.mean(stats[:, 0], axis=0)
    spread = stats[:, 0] - row_mean[None, :]
    row_m2 = jnp.sum(stats[:, 1], axis=0) + width * jnp.sum(spread * spread, axis=0)
    row_scale = lax.rsqrt(row_m2 / D + epsilon)[:, None]
    normed = (widened - row_mean[:, None]) * row_scale
    gain_wide = norm_gain.astype(jnp.float32)
    hidden_local = (normed * gain_wide).astype(jnp.bfloat16)
    hidden_all = spread_quarter(hidden_local)
    cot_all = spread_quarter(cotangent)
    projected = lax.dot_general(
        qkv_flat, hidden_all, contract_cols, preferred_element_type=jnp.float32
    )
    projected = lax.psum_scatter(projected, "dp", scatter_dimension=1, tiled=True)
    projected = projected.astype(jnp.bfloat16).reshape(3, head_slice, HEADS, ROWS)
    up_input = lax.dot_general(
        up_weight, hidden_all, contract_cols, preferred_element_type=jnp.float32
    )
    up_input = lax.psum_scatter(up_input, "dp", scatter_dimension=1, tiled=True)
    activated, gelu_slope = gelu_pair(up_input)
    up_output = activated.astype(jnp.bfloat16)
    queries = projected[0].reshape(head_slice, ITEMS, TQ)
    keyvals = to_items(projected[1:])
    query_heads, pair_heads = (
        lax.all_to_all(queries, "mp", split_axis=1, concat_axis=0, tiled=True),
        lax.all_to_all(keyvals, "mp", split_axis=1, concat_axis=0, tiled=True),
    )
    attended, stored = attend(query_heads, pair_heads)
    head_rows = lax.all_to_all(attended, "mp", split_axis=0, concat_axis=1, tiled=True).reshape(
        head_slice * HEADS, ROWS
    )
    head_rows_all = lax.all_gather(head_rows, "dp", axis=1, tiled=True)
    up_output_all = lax.all_gather(up_output, "dp", axis=1, tiled=True)
    branch = lax.dot_general(
        head_rows_all, head_flat, contract_rows, preferred_element_type=jnp.float32
    ) + lax.dot_general(
        up_output_all, down_weight, contract_rows, preferred_element_type=jnp.float32
    )
    branch_local = gather_quarter(branch, rows)
    mixed = (widened + branch_local).astype(jnp.bfloat16)
    down_grad = blockwise_grad(up_output_all, cot_all, n_dp)
    head_grad = blockwise_grad(head_rows_all, cot_all, n_dp)
    up_back = lax.dot_general(
        down_weight, cot_all, contract_cols, preferred_element_type=jnp.float32
    )
    up_back = lax.psum_scatter(up_back, "dp", scatter_dimension=1, tiled=True)
    up_upstream = (up_back * gelu_slope).astype(jnp.bfloat16)
    head_upstream = lax.dot_general(
        head_flat, cot_all, contract_cols, preferred_element_type=jnp.float32
    )
    head_upstream = lax.psum_scatter(head_upstream, "dp", scatter_dimension=1, tiled=True)
    head_upstream = head_upstream.astype(jnp.bfloat16).reshape(head_slice, ITEMS, TQ)
    upstream = lax.all_to_all(head_upstream, "mp", split_axis=1, concat_axis=0, tiled=True)
    query_grad, pair_grad = attend_back(upstream, stored)
    query_local, pair_local = (
        lax.all_to_all(query_grad, "mp", split_axis=0, concat_axis=1, tiled=True),
        lax.all_to_all(pair_grad, "mp", split_axis=0, concat_axis=1, tiled=True),
    )
    proj_grad = jnp.concatenate(
        [query_local.reshape(1, head_slice, HEADS, ROWS), from_items(pair_local)], axis=0
    )
    proj_grad = proj_grad.reshape(3 * head_slice * HEADS, ROWS)
    proj_grad_all = lax.all_gather(proj_grad, "dp", axis=1, tiled=True)
    up_upstream_all = lax.all_gather(up_upstream, "dp", axis=1, tiled=True)
    qkv_grad = blockwise_grad(proj_grad_all, hidden_all, n_dp)
    up_grad = blockwise_grad(up_upstream_all, hidden_all, n_dp)
    input_partial = lax.dot_general(
        proj_grad_all, qkv_flat, contract_rows, preferred_element_type=jnp.float32
    ) + lax.dot_general(
        up_upstream_all, up_weight, contract_rows, preferred_element_type=jnp.float32
    )
    input_local = gather_quarter(input_partial, rows)
    scaled = input_local * gain_wide
    plain_sum, cross_sum = lax.psum(
        (jnp.sum(scaled, axis=1), jnp.sum(scaled * normed, axis=1)), "mp"
    )
    tokens_grad = row_scale * (scaled - plain_sum[:, None] / D - normed * (cross_sum[:, None] / D))
    tokens_grad = tokens_grad + cotangent.astype(jnp.float32)
    gain_piece = jnp.sum(input_local * normed, axis=0)
    gain_grad = lax.psum(gain_piece, "dp")
    return (
        mixed,
        tokens_grad,
        qkv_grad.reshape(qkv_weight.shape),
        head_grad.reshape(head_weight.shape),
        up_grad,
        down_grad,
        gain_grad,
    )


def solution(mesh):
    in_specs = (
        P("dp", "mp"),
        P("mp"),
        P(None, "mp", None, "dp"),
        P("mp", None, "dp"),
        P("mp", "dp"),
        P("mp", "dp"),
        P("dp", "mp"),
    )
    out_specs = (
        P("dp", "mp"),
        P("dp", "mp"),
        P(None, "mp", None, "dp"),
        P("mp", None, "dp"),
        P("mp", "dp"),
        P("mp", "dp"),
        P("mp"),
    )
    return jax.shard_map(shards, mesh=mesh, in_specs=in_specs, out_specs=out_specs, check_vma=False)
```

profile of v0, /device:TPU:0, one launch (start us, length us, event | category | flops | bytes accessed | tf_op | source)
XLA Modules:
  0.0 604.6 jit_solution(15431614046644285964)
XLA Ops:
  13.6 31.0 %all-gather.3 = f32[8,2,128]{2,1,0:T(2,128)S(1)} all-gather(f32[1,2,128]{2,1,0:T(2,128)S(1)} %maximum_bitcast_fusion), channel_id=2, replica_groups=mesh['dp'=4,'mp'=8] {'mp'}, dimensions={0}, use_global_device_ids=true | all-gather | bytes 9216 | tf_op jit(solution)/shard_map/all_gather | solution.py:170
  47.1 21.2 %all-gather.18.cloned.1.call-done = bf16[1024,768]{1,0:T(8,128)(2,1)} async-done(((bf16[128,768]{1,0:T(8,128)(2,1)}), bf16[1024,768]{1,0:T(8,128)(2,1)}) %all-gather.18.cloned.1.call-update) | async-done | bytes 1572880 | tf_op jit(solution)/shard_map/all_gather | solution.py:127
  74.6 40.2 %all-gather.16.cloned.1.call-done = bf16[1024,768]{1,0:T(8,128)(2,1)} async-done(((bf16[128,768]{1,0:T(8,128)(2,1)}), bf16[1024,768]{1,0:T(8,128)(2,1)}) %all-gather.16.cloned.1.call-update) | async-done | bytes 1572880 | tf_op jit(solution)/shard_map/all_gather | solution.py:127
  123.0 7.3 %fusion.110 = f32[1536,512]{0,1:T(8,128)} fusion(bf16[1536,1536]{1,0:T(8,128)(2,1)} %param.12, bf16[512,1536]{1,0:T(8,128)(2,1)} %bitcast.239), kind=kOutput, calls=%fused_computation.162 | convolution fusion | flops 2415919104 | bytes 9437184 | tf_op jit(solution)/shard_map/dot_general | solution.py:212
  130.3 9.7 %reduce-scatter.13.cloned.1.call-done = f32[384,128]{1,0:T(8,128)} async-done(((f32[384,512]{1,0:T(8,128)}), f32[384,128]{1,0:T(8,128)}) %reduce-scatter.13.cloned.1.call-update) | async-done | bytes 196624 | tf_op jit(solution)/shard_map/reduce_scatter | solution.py:220
  149.0 5.5 all-to-all-start.3
  154.5 21.7 %reduce-scatter.7.cloned.1.call-done = f32[1152,128]{0,1:T(8,128)} async-done(((f32[1152,512]{0,1:T(8,128)}), f32[1152,128]{0,1:T(8,128)}) %reduce-scatter.7.cloned.1.call-update) | async-done | bytes 589840 | tf_op jit(solution)/shard_map/reduce_scatter | solution.py:183
  187.8 5.7 all-to-all-start.1
  203.7 4.3 all-to-all-start
  208.1 7.2 %convolution_bitcast_fusion = f32[1536,512]{0,1:T(8,128)} fusion(bf16[512,1536]{1,0:T(8,128)(2,1)} %bitcast.237, bf16[1536,1536]{1,0:T(8,128)(2,1)} %param.11), kind=kOutput, calls=%fused_computation.24 | convolution fusion | flops 2415919104 | bytes 9437184 | tf_op jit(solution)/shard_map/dot_general | solution.py:185
  269.8 4.4 all-to-all-start.4
  274.2 4.2 bitcast_reduce_fusion
  284.1 6.0 all-to-all-start.5
  297.1 29.3 %all-to-all-done.5 = bf16[128,24,2,128]{3,1,2,0:T(8,128)(2,1)} async-done(((bf16[128,24,2,128]{3,1,2,0:T(8,128)(2,1)}), bf16[128,24,2,128]{3,1,2,0:T(8,128)(2,1)}, u32[]{:S(2)}, u32[]{:S(2)}) %all-to-all-start.5) | async-done | bytes 1572896 | tf_op jit(solution)/shard_map/all_to_all | solution.py:226
  338.1 12.2 %all-gather.12.cloned.1.call-done = bf16[1152,512]{1,0:T(8,128)(2,1)} async-done(((bf16[1152,128]{1,0:T(8,128)(2,1)}), bf16[1152,512]{1,0:T(8,128)(2,1)}) %all-gather.12.cloned.1.call-update) | async-done | bytes 1179664 | tf_op jit(solution)/shard_map/all_gather | solution.py:232
  350.3 5.2 fusion.109
  355.4 16.7 %all-gather.14.cloned.1.call-done = bf16[1536,512]{0,1:T(8,128)(2,1)} async-done(((bf16[1536,128]{0,1:T(8,128)(2,1)}), bf16[1536,512]{0,1:T(8,128)(2,1)}) %all-gather.14.cloned.1.call-update) | async-done | bytes 1572880 | tf_op jit(solution)/shard_map/all_gather | solution.py:233
  372.1 8.0 %convolution_add_fusion.1 = f32[512,1536]{1,0:T(8,128)} fusion(f32[512,1536]{1,0:T(8,128)} %fusion.109, bf16[1536,512]{0,1:T(8,128)(2,1)} %all-gather.14.cloned.1.call-done, bf16[1536,1536]{1,0:T(8,128)(2,1)} %param.11), kind=kOutput, calls=%fused_computation.26 | convolution fusion | flops 2416705536 | bytes 12582912 | tf_op jit(solution)/shard_map/dot_general | solution.py:238
  394.5 5.5 all-to-all-start.2
  403.2 4.1 all-to-all-done.2
  409.8 6.3 %all_gather.34 = bf16[384,512]{1,0:T(8,128)(2,1)S(1)} all-gather(bf16[384,128]{1,0:T(8,128)(2,1)S(1)} %reshape.183), channel_id=1, replica_groups=mesh['dp'=4,'mp'=8] {'dp'}, dimensions={1}, use_global_device_ids=true | all-gather | bytes 491520 | tf_op jit(solution)/shard_map/all_gather | solution.py:201
  421.7 5.3 fusion.107
  437.4 4.0 fusion.13
  452.3 5.9 add_convert_fusion
  458.2 5.0 add_convert_fusion.1
  465.5 4.0 fusion.5
  472.2 4.6 collective-permute-start.3
  476.8 6.3 %fusion.3 = bf16[1152,1536]{1,0:T(8,128)(2,1)} fusion(f32[1152,1536]{1,0:T(8,128)} %fusion.5, bf16[128,1536]{0,1:T(8,128)(2,1)} %bitcast.211, bf16[1152,512]{1,0:T(8,128)(2,1)} %all-gather.12.cloned.1.call-done), kind=kOutput, calls=%fused_computation.6 | convolution fusion | flops 460062720 | bytes 11304960 | tf_op jit(solution)/shard_map/dot_general | solution.py:147
  483.1 77.0 %reduce-scatter.11.cloned.1.call-done = f32[1,128,768]{2,1,0:T(8,128)} async-done(((f32[8,128,768]{2,1,0:T(8,128)}), f32[1,128,768]{2,1,0:T(8,128)}) %reduce-scatter.11.cloned.1.call-update) | async-done | bytes 393232 | tf_op jit(solution)/shard_map/reduce_scatter | solution.py:138
  560.1 4.5 collective-permute-start.1
  566.4 6.8 %psum.23 = f32[768]{0:T(1024)} all-reduce(f32[768]{0:T(1024)S(1)} %get-tuple-element.9), channel_id=1, replica_groups=mesh['dp'=4,'mp'=8] {'dp'}, use_global_device_ids=true, to_apply=%region_27.0 | all-reduce | flops 768 | bytes 6144 | tf_op jit(solution)/shard_map/psum | solution.py:249
  573.2 20.9 %all-reduce = (f32[128]{0:T(128)}, f32[128]{0:T(128)}) all-reduce(f32[128]{0:T(128)} %get-tuple-element.10, f32[128]{0:T(128)} %get-tuple-element.11), channel_id=1, replica_groups=mesh['dp'=4,'mp'=8] {'mp'}, use_global_device_ids=true, to_apply=%region_25.0 | all-reduce | flops 256 | bytes 2048 | tf_op jit(solution)/shard_map/psum | solution.py:243
  (223 shorter events, 189.8 us)
Async XLA Ops:
  7.2 110.9 %copy-start = (bf16[3,16,24,1536]{3,2,1,0:T(8,128)(2,1)S(1)}, bf16[3,16,24,1536]{3,2,1,0:T(8,128)(2,1)}, u32[]{:S(2)}) copy-start(bf16[3,16,24,1536]{3,2,1,0:T(8,128)(2,1)} %param.9) | copy-start | bytes 10616836
  7.2 61.2 %all-gather.18.cloned.1.call-start = ((), (), s32[]{:S(2)}) async-start(), calls=%async_computation.22 | async-start | bytes 1769472 | tf_op jit(solution)/shard_map/all_gather | solution.py:127
  7.2 3.4 collective-permute-start.2
  10.6 104.1 %all-gather.16.cloned.1.call-start = ((), (), s32[]{:S(2)}) async-start(), calls=%async_computation.21 | async-start | bytes 1769472 | tf_op jit(solution)/shard_map/all_gather | solution.py:127
  44.6 26.8 %copy-start.34 = (f32[128]{0:T(128)}, f32[128]{0:T(128)S(1)}, u32[]{:S(2)}) copy-start(f32[128]{0:T(128)S(1)} %broadcast_multiply_fusion.8) | copy-start | bytes 1540
  44.6 26.8 %copy-start.36 = (f32[128]{0:T(128)}, f32[128]{0:T(128)S(1)}, u32[]{:S(2)}) copy-start(f32[128]{0:T(128)S(1)} %add_rsqrt_fusion.2) | copy-start | bytes 1540
  45.7 1.3 collective-permute-start
  47.1 92.9 %reduce-scatter.13.cloned.1.call-start = ((), (), s32[]{:S(2)}) async-start(), calls=%async_computation.16 | async-start | bytes 983040 | tf_op jit(solution)/shard_map/reduce_scatter | solution.py:220
  74.6 101.7 %reduce-scatter.7.cloned.1.call-start = ((), (), s32[]{:S(2)}) async-start(), calls=%async_computation.12 | async-start | bytes 2949120 | tf_op jit(solution)/shard_map/reduce_scatter | solution.py:183
  122.9 211.6 %reduce-scatter.15.cloned.1.call-start = ((), (), s32[]{:S(2)}) async-start(), calls=%async_computation.18 | async-start | bytes 3932160 | tf_op jit(solution)/shard_map/reduce_scatter | solution.py:215
  149.0 38.8 %all-to-all-start.3 = ((bf16[8,2,3072]{2,1,0:T(2,128)(2,1)}), bf16[8,2,3072]{2,1,0:T(2,128)(2,1)}, u32[]{:S(2)}, u32[]{:S(2)}) async-start(bf16[8,2,3072]{2,1,0:T(2,128)(2,1)} %reshape.215), calls=%async_computation.7 | async-start | bytes 196608 | tf_op jit(solution)/shard_map/all_to_all | solution.py:222
  187.8 13.0 %all-to-all-start.1 = ((bf16[8,2,3072]{2,1,0:T(2,128)(2,1)}), bf16[8,2,3072]{2,1,0:T(2,128)(2,1)}, u32[]{:S(2)}, u32[]{:S(2)}) async-start(bf16[8,2,3072]{2,1,0:T(2,128)(2,1)} %reshape.211), calls=%async_computation.2 | async-start | bytes 196608 | tf_op jit(solution)/shard_map/all_to_all | solution.py:194
  203.7 40.6 %all-to-all-start = ((bf16[16,192,2,128]{3,2,0,1:T(2,128)(2,1)}), bf16[16,192,2,128]{3,2,0,1:T(2,128)(2,1)}, u32[]{:S(2)}, u32[]{:S(2)}) async-start(bf16[16,192,2,128]{3,2,0,1:T(2,128)(2,1)} %bitcast.205), calls=%async_computation.1 | async-start | bytes 3145728 | tf_op jit(solution)/shard_map/all_to_all | solution.py:195
  208.0 126.5 %reduce-scatter.9.cloned.1.call-start = ((), (), s32[]{:S(2)}) async-start(), calls=%async_computation.13 | async-start | bytes 3932160 | tf_op jit(solution)/shard_map/reduce_scatter | solution.py:188
  269.8 14.3 %all-to-all-start.4 = ((bf16[8,2,3072]{2,1,0:T(2,128)(2,1)}), bf16[8,2,3072]{2,1,0:T(2,128)(2,1)}, u32[]{:S(2)}, u32[]{:S(2)}) async-start(bf16[8,2,3072]{2,1,0:T(2,128)(2,1)} %reshape.217), calls=%async_computation.8 | async-start | bytes 196608 | tf_op jit(solution)/shard_map/all_to_all | solution.py:225
  284.1 42.3 %all-to-all-start.5 = ((bf16[128,24,2,128]{3,1,2,0:T(8,128)(2,1)}), bf16[128,24,2,128]{3,1,2,0:T(8,128)(2,1)}, u32[]{:S(2)}, u32[]{:S(2)}) async-start(bf16[128,24,2,128]{3,1,2,0:T(8,128)(2,1)} %copy.197), calls=%async_computation.9 | async-start | bytes 3145728 | tf_op jit(solution)/shard_map/all_to_all | solution.py:226
  290.1 60.2 %all-gather.12.cloned.1.call-start = ((), (), s32[]{:S(2)}) async-start(), calls=%async_computation.17 | async-start | bytes 1474560 | tf_op jit(solution)/shard_map/all_gather | solution.py:232
  334.4 37.7 %all-gather.14.cloned.1.call-start = ((), (), s32[]{:S(2)}) async-start(), calls=%async_computation.19 | async-start | bytes 1966080 | tf_op jit(solution)/shard_map/all_gather | solution.py:233
  337.2 84.6 %all-gather.10.cloned.1.call-start = ((), (), s32[]{:S(2)}) async-start(), calls=%async_computation.14 | async-start | bytes 1966080 | tf_op jit(solution)/shard_map/all_gather | solution.py:202
  337.9 134.3 %reduce-scatter.17.cloned.1.call-start = ((), (), s32[]{:S(2)}) async-start(), calls=%async_computation.20 | async-start | bytes 3538944 | tf_op jit(solution)/shard_map/reduce_scatter | solution.py:138
  390.4 9.7 %copy-start.7 = (bf16[1024,768]{1,0:T(8,128)(2,1)S(1)}, bf16[1024,768]{1,0:T(8,128)(2,1)}, u32[]{:S(2)}) copy-start(bf16[1024,768]{1,0:T(8,128)(2,1)} %all-gather.16.cloned.1.call-done) | copy-start | bytes 4718596
  394.5 12.8 %all-to-all-start.2 = ((bf16[8,2,3072]{2,1,0:T(2,128)(2,1)}), bf16[8,2,3072]{2,1,0:T(2,128)(2,1)}, u32[]{:S(2)}, u32[]{:S(2)}) async-start(bf16[8,2,3072]{2,1,0:T(2,128)(2,1)} %reshape.213), calls=%async_computation.3 | async-start | bytes 196608 | tf_op jit(solution)/shard_map/all_to_all | solution.py:198
  400.1 160.0 %reduce-scatter.11.cloned.1.call-start = ((), (), s32[]{:S(2)}) async-start(), calls=%async_computation.15 | async-start | bytes 3538944 | tf_op jit(solution)/shard_map/reduce_scatter | solution.py:138
  400.4 47.5 %copy-start.10 = (bf16[1,128,2,768]{1,3,2,0:T(8,128)(2,1)}, bf16[1,128,2,768]{1,3,2,0:T(8,128)(2,1)S(1)}, u32[]{:S(2)}) copy-start(bf16[1,128,2,768]{1,3,2,0:T(8,128)(2,1)S(1)} %copy.206) | copy-start | bytes 1179652
  403.2 12.9 %copy-start.11 = (bf16[1,128,2,768]{1,3,2,0:T(8,128)(2,1)S(1)}, bf16[1,128,2,768]{1,3,2,0:T(8,128)(2,1)}, u32[]{:S(2)}) copy-start(bf16[1,128,2,768]{1,3,2,0:T(8,128)(2,1)} %copy.210) | copy-start | bytes 1179652
  409.8 8.2 %copy-start.13 = (bf16[1,128,2,768]{1,3,2,0:T(8,128)(2,1)S(1)}, bf16[1,128,2,768]{1,3,2,0:T(8,128)(2,1)}, u32[]{:S(2)}) copy-start(bf16[1,128,2,768]{1,3,2,0:T(8,128)(2,1)} %copy.209) | copy-start | bytes 1179652
  416.1 11.0 %copy-start.17 = (bf16[384,512]{1,0:T(8,128)(2,1)}, bf16[384,512]{1,0:T(8,128)(2,1)S(1)}, u32[]{:S(2)}) copy-start(bf16[384,512]{1,0:T(8,128)(2,1)S(1)} %all_gather.34) | copy-start | bytes 1179652
  472.2 92.3 %copy-start.35 = (f32[128]{0:T(128)S(1)}, f32[128]{0:T(128)}, u32[]{:S(2)}) copy-start(f32[128]{0:T(128)} %copy-done.34) | copy-start | bytes 1540
  472.2 92.3 %copy-start.37 = (f32[128]{0:T(128)S(1)}, f32[128]{0:T(128)}, u32[]{:S(2)}) copy-start(f32[128]{0:T(128)} %copy-done.36) | copy-start | bytes 1540
  472.2 92.3 %collective-permute-start.3 = (f32[128,768]{1,0:T(8,128)}, f32[128,768]{1,0:T(8,128)}, u32[]{:S(2)}, u32[]{:S(2)}) collective-permute-start(f32[128,768]{1,0:T(8,128)} %bitcast.249), channel_id=1, source_target_pairs={{0,0},{1,1},{2,8},{3,9},{4,16},{5,17},{6,24},{7,25},{8,2},{9,3},{1... | collective-permute-start | bytes 1179656 | tf_op jit(solution)/shard_map/ppermute | solution.py:120
  476.8 120.9 %copy-start.1 = (bf16[3,16,24,1536]{3,2,1,0:T(8,128)(2,1)S(1)}, bf16[3,16,24,1536]{3,2,1,0:T(8,128)(2,1)}, u32[]{:S(2)}) copy-start(bf16[3,16,24,1536]{3,2,1,0:T(8,128)(2,1)} %param.9) | copy-start | bytes 10616836
  560.1 35.3 %collective-permute-start.1 = (f32[128,768]{1,0:T(8,128)}, f32[128,768]{1,0:T(8,128)}, u32[]{:S(2)}, u32[]{:S(2)}) collective-permute-start(f32[128,768]{1,0:T(8,128)} %bitcast.250), channel_id=1, source_target_pairs={{0,0},{1,1},{2,8},{3,9},{4,16},{5,17},{6,24},{7,25},{8,2},{9,3},{1... | collective-permute-start | bytes 1179656 | tf_op jit(solution)/shard_map/ppermute | solution.py:120
  (27 other events, 59.8 us)
Sparse Core Ops, SparseCore 0:
  10.7 57.5 all-gather.17
  70.5 44.1 all-gather.15
  117.9 22.0 reduce-scatter.12
  143.1 33.0 reduce-scatter.6
  179.2 37.9 reduce-scatter.14
  220.3 37.9 reduce-scatter.8
  334.6 15.6 all-gather.11
  352.4 19.6 all-gather.13
  374.3 19.6 all-gather.9
  398.0 74.2 reduce-scatter.16
  475.8 84.2 reduce-scatter.10
where the time goes:
time: 616 us; the launch traced here: 605 us
  waiting for transfers between devices  242 us (39%)
  local copies, waits for them, and re-layouts  110 us (18%)
  matrix products  97.6 us (16%)
  blocking collectives  65 us (11%)
  starting transfers between devices  45.8 us (7%)
  other arithmetic  29.7 us (5%)
  between operations  14.9 us (2%)
    reduce_scatter x2, waiting for transfers between devices, gather_quarter(): summed = lax.psum_scatter(pieces, 'mp', scatter_dimension=0, tiled=True)  79.7 us
    all_gather x2, waiting for transfers between devices, spread_quarter(): pieces = lax.all_gather(swap(block), 'mp', axis=0, tiled=False)  61.4 us
    dot_general x16, matrix products, blockwise_grad(): jnp.dot(left[:, block * rows:(block + 1) * rows], right[block * rows:(blo...  43.7 us
    all_gather x1, blocking collectives, shards(): lax.all_gather(jnp.stack([block_mean, block_m2]), 'mp', axis=0, tiled=False)  31 us
    all_to_all x1, waiting for transfers between devices, shards(): lax.all_to_all(pair_grad, 'mp', split_axis=0, concat_axis=1, tiled=True)  29.3 us
    unnamed x86, local copies, waits for them, and re-layouts  24.5 us
    reduce_scatter x1, waiting for transfers between devices, shards(): lax.psum_scatter(projected, 'dp', scatter_dimension=1, tiled=True)  21.7 us
    psum x1, blocking collectives, shards(): lax.psum((jnp.sum(scaled, axis=1), jnp.sum(scaled * normed, axis=1)), 'mp')  20.9 us
  transfers between devices with their start and end apart: 21, of which 12 were waited for; matrix products, arithmetic and copies ran while one was open for 37% of the time, Pallas kernels for 0%

commit v1 on v0

--- a/solution.py
+++ b/solution.py
@@ -229,8 +229,11 @@
         [query_local.reshape(1, head_slice, HEADS, ROWS), from_items(pair_local)], axis=0
     )
     proj_grad = proj_grad.reshape(3 * head_slice * HEADS, ROWS)
-    proj_grad_all = lax.all_gather(proj_grad, "dp", axis=1, tiled=True)
-    up_upstream_all = lax.all_gather(up_upstream, "dp", axis=1, tiled=True)
+    proj_grad_all, up_upstream_all = jnp.split(
+        lax.all_gather(jnp.concatenate([proj_grad, up_upstream], axis=0), "dp", axis=1, tiled=True),
+        [proj_grad.shape[0]],
+        axis=0,
+    )
     qkv_grad = blockwise_grad(proj_grad_all, hidden_all, n_dp)
     up_grad = blockwise_grad(up_upstream_all, hidden_all, n_dp)
     input_partial = lax.dot_general(

time: 616 us -> 608 us (0.987)
  matrix products: 97.6 us -> 89.4 us
    all_gather x2 -> x1, waiting for transfers between devices: 28.8 us -> 23.6 us  [shards(): lax.all_gather(jnp.concatenate([proj_grad, up_upstream], axis=0), 'dp', a...]
    unnamed x86 -> x78, local copies, waits for them, and re-layouts: 24.5 us -> 24.3 us
  transfers between devices with their start and end apart: 21 -> 20, of which waited for: 12 -> 11; matrix products, arithmetic and copies ran while one was open for 37% -> 36% of each run, Pallas kernels for 0% -> 0%
where the time goes in v1:
time: 608 us; the launch traced here: 596 us
  waiting for transfers between devices  236 us (39%)
  local copies, waits for them, and re-layouts  114 us (19%)
  matrix products  89.4 us (15%)
  blocking collectives  64.9 us (11%)
  starting transfers between devices  45.7 us (8%)
  other arithmetic  31.6 us (5%)
  between operations  15.2 us (2%)
    reduce_scatter x2, waiting for transfers between devices, gather_quarter(): summed = lax.psum_scatter(pieces, 'mp', scatter_dimension=0, tiled=True)  80.1 us
    all_gather x2, waiting for transfers between devices, spread_quarter(): pieces = lax.all_gather(swap(block), 'mp', axis=0, tiled=False)  61.4 us
    dot_general x16, matrix products, blockwise_grad(): jnp.dot(left[:, block * rows:(block + 1) * rows], right[block * rows:(blo...  38.8 us
    all_gather x1, blocking collectives, shards(): lax.all_gather(jnp.stack([block_mean, block_m2]), 'mp', axis=0, tiled=False)  31 us
    all_to_all x1, waiting for transfers between devices, shards(): lax.all_to_all(pair_grad, 'mp', split_axis=0, concat_axis=1, tiled=True)  26.7 us
    unnamed x78, local copies, waits for them, and re-layouts  24.3 us
    all_gather x1, waiting for transfers between devices, shards(): lax.all_gather(jnp.concatenate([proj_grad, up_upstream], axis=0), 'dp', a...  23.6 us
    reduce_scatter x1, waiting for transfers between devices, shards(): lax.psum_scatter(projected, 'dp', scatter_dimension=1, tiled=True)  21.7 us
  transfers between devices with their start and end apart: 20, of which 11 were waited for; matrix products, arithmetic and copies ran while one was open for 36% of the time, Pallas kernels for 0%

profile of v1, /device:TPU:0, one launch (start us, length us, event | category | flops | bytes accessed | tf_op | source)
XLA Modules:
  0.0 596.5 jit_solution(5633966911684042112)
XLA Ops:
  13.5 31.0 %all-gather.3 = f32[8,2,128]{2,1,0:T(2,128)S(1)} all-gather(f32[1,2,128]{2,1,0:T(2,128)S(1)} %maximum_bitcast_fusion), channel_id=2, replica_groups=mesh['dp'=4,'mp'=8] {'mp'}, dimensions={0}, use_global_device_ids=true | all-gather | bytes 9216 | tf_op jit(solution)/shard_map/all_gather | solution.py:170
  47.2 21.2 %all-gather.15.cloned.1.call-done = bf16[1024,768]{1,0:T(8,128)(2,1)} async-done(((bf16[128,768]{1,0:T(8,128)(2,1)}), bf16[1024,768]{1,0:T(8,128)(2,1)}) %all-gather.15.cloned.1.call-update) | async-done | bytes 1572880 | tf_op jit(solution)/shard_map/all_gather | solution.py:127
  74.6 40.2 %all-gather.13.cloned.1.call-done = bf16[1024,768]{1,0:T(8,128)(2,1)} async-done(((bf16[128,768]{1,0:T(8,128)(2,1)}), bf16[1024,768]{1,0:T(8,128)(2,1)}) %all-gather.13.cloned.1.call-update) | async-done | bytes 1572880 | tf_op jit(solution)/shard_map/all_gather | solution.py:127
  123.0 7.3 %fusion.112 = f32[1536,512]{0,1:T(8,128)} fusion(bf16[1536,1536]{1,0:T(8,128)(2,1)} %param.12, bf16[512,1536]{1,0:T(8,128)(2,1)} %bitcast.237), kind=kOutput, calls=%fused_computation.165 | convolution fusion | flops 2415919104 | bytes 9437184 | tf_op jit(solution)/shard_map/dot_general | solution.py:212
  130.3 9.7 %reduce-scatter.13.cloned.1.call-done = f32[384,128]{1,0:T(8,128)} async-done(((f32[384,512]{1,0:T(8,128)}), f32[384,128]{1,0:T(8,128)}) %reduce-scatter.13.cloned.1.call-update) | async-done | bytes 196624 | tf_op jit(solution)/shard_map/reduce_scatter | solution.py:220
  149.0 5.5 all-to-all-start.3
  154.5 21.7 %reduce-scatter.7.cloned.1.call-done = f32[1152,128]{0,1:T(8,128)} async-done(((f32[1152,512]{0,1:T(8,128)}), f32[1152,128]{0,1:T(8,128)}) %reduce-scatter.7.cloned.1.call-update) | async-done | bytes 589840 | tf_op jit(solution)/shard_map/reduce_scatter | solution.py:183
  187.8 5.7 all-to-all-start.1
  203.7 4.3 all-to-all-start
  208.1 7.2 %convolution_bitcast_fusion = f32[1536,512]{0,1:T(8,128)} fusion(bf16[512,1536]{1,0:T(8,128)(2,1)} %bitcast.235, bf16[1536,1536]{1,0:T(8,128)(2,1)} %param.11), kind=kOutput, calls=%fused_computation.24 | convolution fusion | flops 2415919104 | bytes 9437184 | tf_op jit(solution)/shard_map/dot_general | solution.py:185
  240.1 4.2 all-to-all-done
  269.8 4.4 all-to-all-start.4
  274.2 4.2 bitcast_reduce_fusion
  284.0 6.0 all-to-all-start.5
  299.6 26.7 %all-to-all-done.5 = bf16[128,24,2,128]{3,1,2,0:T(8,128)(2,1)} async-done(((bf16[128,24,2,128]{3,1,2,0:T(8,128)(2,1)}), bf16[128,24,2,128]{3,1,2,0:T(8,128)(2,1)}, u32[]{:S(2)}, u32[]{:S(2)}) %all-to-all-start.5) | async-done | bytes 1572896 | tf_op jit(solution)/shard_map/all_to_all | solution.py:226
  339.1 23.6 %all-gather.11.cloned.1.call-done = bf16[2688,512]{0,1:T(8,128)(2,1)} async-done(((bf16[2688,128]{0,1:T(8,128)(2,1)}), bf16[2688,512]{0,1:T(8,128)(2,1)}) %all-gather.11.cloned.1.call-update) | async-done | bytes 2752528 | tf_op jit(solution)/shard_map/all_gather | solution.py:233
  366.3 6.7 %convolution_add_fusion.1 = f32[512,1536]{1,0:T(8,128)} fusion(f32[512,1536]{1,0:T(8,128)S(1)} %fusion.30, bf16[1536,1536]{1,0:T(8,128)(2,1)} %param.11, bf16[2688,512]{0,1:T(8,128)(2,1)S(1)} %copy-done.7), kind=kOutput, calls=%fused_computation.26 | convolution fusion | flops 2416705536 | bytes 12582912 | tf_op jit(solution)/shard_map/dot_general | solution.py:241
  390.2 5.5 all-to-all-start.2
  398.9 5.5 all-to-all-done.2
  406.9 6.4 %all_gather.31 = bf16[384,512]{1,0:T(8,128)(2,1)S(1)} all-gather(bf16[384,128]{1,0:T(8,128)(2,1)S(1)} %reshape.183), channel_id=1, replica_groups=mesh['dp'=4,'mp'=8] {'dp'}, dimensions={1}, use_global_device_ids=true | all-gather | bytes 491520 | tf_op jit(solution)/shard_map/all_gather | solution.py:201
  418.9 5.1 fusion.110
  426.7 3.9 reshape.185
  434.4 4.1 fusion.13
  442.8 4.1 add_convert_fusion
  453.6 4.0 fusion.5
  457.6 3.9 add_convert_fusion.1
  464.6 4.6 collective-permute-start.3
  469.2 6.3 %fusion.3 = bf16[1152,1536]{1,0:T(8,128)(2,1)} fusion(f32[1152,1536]{1,0:T(8,128)} %fusion.5, bf16[128,1536]{0,1:T(8,128)(2,1)} %bitcast.209, bf16[2688,512]{0,1:T(8,128)(2,1)} %all-gather.11.cloned.1.call-done), kind=kOutput, calls=%fused_computation.6 | convolution fusion | flops 460062720 | bytes 11304960 | tf_op jit(solution)/shard_map/dot_general | solution.py:147
  475.4 77.0 %reduce-scatter.11.cloned.1.call-done = f32[1,128,768]{2,1,0:T(8,128)} async-done(((f32[8,128,768]{2,1,0:T(8,128)}), f32[1,128,768]{2,1,0:T(8,128)}) %reduce-scatter.11.cloned.1.call-update) | async-done | bytes 393232 | tf_op jit(solution)/shard_map/reduce_scatter | solution.py:138
  552.4 4.5 collective-permute-start.1
  558.7 6.8 %psum.23 = f32[768]{0:T(1024)} all-reduce(f32[768]{0:T(1024)S(1)} %get-tuple-element.9), channel_id=1, replica_groups=mesh['dp'=4,'mp'=8] {'dp'}, use_global_device_ids=true, to_apply=%region_27.0 | all-reduce | flops 768 | bytes 6144 | tf_op jit(solution)/shard_map/psum | solution.py:252
  565.5 20.7 %all-reduce = (f32[128]{0:T(128)}, f32[128]{0:T(128)S(1)}) all-reduce(f32[128]{0:T(128)} %get-tuple-element.10, f32[128]{0:T(128)} %get-tuple-element.11), channel_id=1, replica_groups=mesh['dp'=4,'mp'=8] {'mp'}, use_global_device_ids=true, to_apply=%region_25.0 | all-reduce | flops 256 | bytes 2048 | tf_op jit(solution)/shard_map/psum | solution.py:246
  (214 shorter events, 189.3 us)
Async XLA Ops:
  7.2 110.9 %copy-start = (bf16[3,16,24,1536]{3,2,1,0:T(8,128)(2,1)S(1)}, bf16[3,16,24,1536]{3,2,1,0:T(8,128)(2,1)}, u32[]{:S(2)}) copy-start(bf16[3,16,24,1536]{3,2,1,0:T(8,128)(2,1)} %param.9) | copy-start | bytes 10616836
  7.2 61.2 %all-gather.15.cloned.1.call-start = ((), (), s32[]{:S(2)}) async-start(), calls=%async_computation.21 | async-start | bytes 1769472 | tf_op jit(solution)/shard_map/all_gather | solution.py:127
  7.2 3.4 collective-permute-start.2
  10.6 104.1 %all-gather.13.cloned.1.call-start = ((), (), s32[]{:S(2)}) async-start(), calls=%async_computation.20 | async-start | bytes 1769472 | tf_op jit(solution)/shard_map/all_gather | solution.py:127
  45.7 1.3 collective-permute-start
  47.1 92.9 %reduce-scatter.13.cloned.1.call-start = ((), (), s32[]{:S(2)}) async-start(), calls=%async_computation.16 | async-start | bytes 983040 | tf_op jit(solution)/shard_map/reduce_scatter | solution.py:220
  74.5 101.7 %reduce-scatter.7.cloned.1.call-start = ((), (), s32[]{:S(2)}) async-start(), calls=%async_computation.12 | async-start | bytes 2949120 | tf_op jit(solution)/shard_map/reduce_scatter | solution.py:183
  122.9 167.1 %reduce-scatter.15.cloned.1.call-start = ((), (), s32[]{:S(2)}) async-start(), calls=%async_computation.17 | async-start | bytes 3932160 | tf_op jit(solution)/shard_map/reduce_scatter | solution.py:215
  149.0 38.8 %all-to-all-start.3 = ((bf16[8,2,3072]{2,1,0:T(2,128)(2,1)}), bf16[8,2,3072]{2,1,0:T(2,128)(2,1)}, u32[]{:S(2)}, u32[]{:S(2)}) async-start(bf16[8,2,3072]{2,1,0:T(2,128)(2,1)} %reshape.215), calls=%async_computation.7 | async-start | bytes 196608 | tf_op jit(solution)/shard_map/all_to_all | solution.py:222
  187.8 13.0 %all-to-all-start.1 = ((bf16[8,2,3072]{2,1,0:T(2,128)(2,1)}), bf16[8,2,3072]{2,1,0:T(2,128)(2,1)}, u32[]{:S(2)}, u32[]{:S(2)}) async-start(bf16[8,2,3072]{2,1,0:T(2,128)(2,1)} %reshape.211), calls=%async_computation.2 | async-start | bytes 196608 | tf_op jit(solution)/shard_map/all_to_all | solution.py:194
  203.7 40.6 %all-to-all-start = ((bf16[16,192,2,128]{3,2,0,1:T(2,128)(2,1)}), bf16[16,192,2,128]{3,2,0,1:T(2,128)(2,1)}, u32[]{:S(2)}, u32[]{:S(2)}) async-start(bf16[16,192,2,128]{3,2,0,1:T(2,128)(2,1)} %bitcast.203), calls=%async_computation.1 | async-start | bytes 3145728 | tf_op jit(solution)/shard_map/all_to_all | solution.py:195
  208.0 82.0 %reduce-scatter.9.cloned.1.call-start = ((), (), s32[]{:S(2)}) async-start(), calls=%async_computation.13 | async-start | bytes 3932160 | tf_op jit(solution)/shard_map/reduce_scatter | solution.py:188
  269.8 14.2 %all-to-all-start.4 = ((bf16[8,2,3072]{2,1,0:T(2,128)(2,1)}), bf16[8,2,3072]{2,1,0:T(2,128)(2,1)}, u32[]{:S(2)}, u32[]{:S(2)}) async-start(bf16[8,2,3072]{2,1,0:T(2,128)(2,1)} %reshape.217), calls=%async_computation.8 | async-start | bytes 196608 | tf_op jit(solution)/shard_map/all_to_all | solution.py:225
  284.0 42.3 %all-to-all-start.5 = ((bf16[128,24,2,128]{3,1,2,0:T(8,128)(2,1)}), bf16[128,24,2,128]{3,1,2,0:T(8,128)(2,1)}, u32[]{:S(2)}, u32[]{:S(2)}) async-start(bf16[128,24,2,128]{3,1,2,0:T(8,128)(2,1)} %copy.201), calls=%async_computation.9 | async-start | bytes 3145728 | tf_op jit(solution)/shard_map/all_to_all | solution.py:226
  290.0 72.7 %all-gather.11.cloned.1.call-start = ((), (), s32[]{:S(2)}) async-start(), calls=%async_computation.18 | async-start | bytes 3440640 | tf_op jit(solution)/shard_map/all_gather | solution.py:233
  338.1 80.8 %all-gather.9.cloned.1.call-start = ((), (), s32[]{:S(2)}) async-start(), calls=%async_computation.14 | async-start | bytes 1966080 | tf_op jit(solution)/shard_map/all_gather | solution.py:202
  338.8 125.7 %reduce-scatter.17.cloned.1.call-start = ((), (), s32[]{:S(2)}) async-start(), calls=%async_computation.19 | async-start | bytes 3538944 | tf_op jit(solution)/shard_map/reduce_scatter | solution.py:138
  381.2 5.8 copy-start.3
  382.1 13.7 %copy-start.6 = (bf16[1024,768]{1,0:T(8,128)(2,1)S(1)}, bf16[1024,768]{1,0:T(8,128)(2,1)}, u32[]{:S(2)}) copy-start(bf16[1024,768]{1,0:T(8,128)(2,1)} %all-gather.13.cloned.1.call-done) | copy-start | bytes 4718596
  390.2 14.2 %all-to-all-start.2 = ((bf16[8,2,3072]{2,1,0:T(2,128)(2,1)}), bf16[8,2,3072]{2,1,0:T(2,128)(2,1)}, u32[]{:S(2)}, u32[]{:S(2)}) async-start(bf16[8,2,3072]{2,1,0:T(2,128)(2,1)} %reshape.213), calls=%async_computation.3 | async-start | bytes 196608 | tf_op jit(solution)/shard_map/all_to_all | solution.py:198
  395.7 156.7 %reduce-scatter.11.cloned.1.call-start = ((), (), s32[]{:S(2)}) async-start(), calls=%async_computation.15 | async-start | bytes 3538944 | tf_op jit(solution)/shard_map/reduce_scatter | solution.py:138
  396.1 50.9 %copy-start.10 = (bf16[1,128,2,768]{1,3,2,0:T(8,128)(2,1)}, bf16[1,128,2,768]{1,3,2,0:T(8,128)(2,1)S(1)}, u32[]{:S(2)}) copy-start(bf16[1,128,2,768]{1,3,2,0:T(8,128)(2,1)S(1)} %copy.211) | copy-start | bytes 1179652
  397.0 16.3 %copy-start.11 = (bf16[1,128,2,768]{1,3,2,0:T(8,128)(2,1)S(1)}, bf16[1,128,2,768]{1,3,2,0:T(8,128)(2,1)}, u32[]{:S(2)}) copy-start(bf16[1,128,2,768]{1,3,2,0:T(8,128)(2,1)} %copy.215) | copy-start | bytes 1179652
  406.4 8.8 %copy-start.13 = (bf16[1,128,2,768]{1,3,2,0:T(8,128)(2,1)S(1)}, bf16[1,128,2,768]{1,3,2,0:T(8,128)(2,1)}, u32[]{:S(2)}) copy-start(bf16[1,128,2,768]{1,3,2,0:T(8,128)(2,1)} %copy.214) | copy-start | bytes 1179652
  413.3 10.7 %copy-start.17 = (bf16[384,512]{1,0:T(8,128)(2,1)}, bf16[384,512]{1,0:T(8,128)(2,1)S(1)}, u32[]{:S(2)}) copy-start(bf16[384,512]{1,0:T(8,128)(2,1)S(1)} %all_gather.31) | copy-start | bytes 1179652
  418.9 5.1 copy-start.26
  442.8 4.2 copy-start.8
  464.6 92.3 %copy-start.31 = (f32[128]{0:T(128)S(1)}, f32[128]{0:T(128)}, u32[]{:S(2)}) copy-start(f32[128]{0:T(128)} %copy-done.30) | copy-start | bytes 1540
  464.6 92.3 %copy-start.33 = (f32[128]{0:T(128)S(1)}, f32[128]{0:T(128)}, u32[]{:S(2)}) copy-start(f32[128]{0:T(128)} %copy-done.32) | copy-start | bytes 1540
  464.6 92.3 %collective-permute-start.3 = (f32[128,768]{1,0:T(8,128)}, f32[128,768]{1,0:T(8,128)}, u32[]{:S(2)}, u32[]{:S(2)}) collective-permute-start(f32[128,768]{1,0:T(8,128)} %bitcast.247), channel_id=1, source_target_pairs={{0,0},{1,1},{2,8},{3,9},{4,16},{5,17},{6,24},{7,25},{8,2},{9,3},{1... | collective-permute-start | bytes 1179656 | tf_op jit(solution)/shard_map/ppermute | solution.py:120
  469.2 120.0 %copy-start.1 = (bf16[3,16,24,1536]{3,2,1,0:T(8,128)(2,1)S(1)}, bf16[3,16,24,1536]{3,2,1,0:T(8,128)(2,1)}, u32[]{:S(2)}) copy-start(bf16[3,16,24,1536]{3,2,1,0:T(8,128)(2,1)} %param.9) | copy-start | bytes 10616836
  552.4 34.5 %collective-permute-start.1 = (f32[128,768]{1,0:T(8,128)}, f32[128,768]{1,0:T(8,128)}, u32[]{:S(2)}, u32[]{:S(2)}) collective-permute-start(f32[128,768]{1,0:T(8,128)} %bitcast.248), channel_id=1, source_target_pairs={{0,0},{1,1},{2,8},{3,9},{4,16},{5,17},{6,24},{7,25},{8,2},{9,3},{1... | collective-permute-start | bytes 1179656 | tf_op jit(solution)/shard_map/ppermute | solution.py:120
  (22 other events, 46.2 us)
Sparse Core Ops, SparseCore 0:
  10.7 57.5 all-gather.14
  70.5 44.1 all-gather.12
  117.9 22.0 reduce-scatter.12
  143.1 33.0 reduce-scatter.6
  179.2 37.9 reduce-scatter.14
  220.3 37.9 reduce-scatter.8
  338.2 24.4 all-gather.10
  364.8 19.6 all-gather.8
  388.7 75.8 reduce-scatter.16
  468.0 84.3 reduce-scatter.10
